TPU v7x, 256 devices: a whole 4x4x8 slice. The times are simulated.
256 devices in a mesh: neuron: 16 (over z, x_hi), tm: 16 (over y, x_lo, core).
Axes of the slice: x: 4 (x_hi: 2, x_lo: 2; x = x_hi * 2 + x_lo), y: 4, z: 8, core: 2. Of those that a mesh axis runs over, the one named last changes fastest.
Arguments:
- signal: bfloat16 [8192, 65536], P('tm', 'neuron'), may hold values from -6 to 6
- readin: bfloat16 [65536, 256], P('neuron'), may hold values from -0.0234375 to 0.0234375
- proj: bfloat16 [256, 512], replicated, may hold values from -0.375 to 0.375
- kernel: float32 [63, 512], replicated, may hold values from -0.75 to 0.75
- gain: float32 [512], replicated, may hold values from 0.5 to 1.5
- w_one: bfloat16 [512, 2048], P(None, 'neuron'), may hold values from -0.25 to 0.25
- w_two: bfloat16 [2048, 512], P('neuron'), may hold values from -0.125 to 0.125
- cotangent: bfloat16 [8192, 512], P('tm'), may hold values from -6 to 6
Outputs:
- denoised: bfloat16 [8192, 512], P('tm')
- grad_readin: float32 [65536, 256], P(('neuron', 'tm'))
- grad_proj: float32 [256, 512], replicated
- grad_kernel: float32 [63, 512], replicated
- grad_gain: float32 [512], replicated
- grad_w_one: float32 [512, 2048], P(None, 'neuron')
- grad_w_two: float32 [2048, 512], P('neuron')
All inputs are finite; a program needn't handle non-finite values.
Results may differ from a plain program's by a relative error of at most 0.0085.
Values may be sent and summed in bfloat16 or wider, within the bound.
No kernel may reach another device: no remote copies, remote signals or barrier semaphores. Data moves between devices by JAX's collectives and lax.ppermute only.
A program may use at most 64 MiB of HBM per device.

v0:
```python
import jax
import jax.numpy as jnp
from jax import lax
from jax.sharding import PartitionSpec as P


def with_halo(block, sides, width):
    for axis, dim in sides:
        count = lax.axis_size(axis)
        forward = [(i, i + 1) for i in range(count - 1)]
        backward = [(target, source) for source, target in forward]
        low = lax.ppermute(
            lax.slice_in_dim(block, block.shape[dim] - width, None, axis=dim), axis, forward
        )
        high = lax.ppermute(lax.slice_in_dim(block, 0, width, axis=dim), axis, backward)
        block = jnp.concatenate([low, block, high], axis=dim)
    return block


def conv_time(padded, kernel, rows):

    def step(index, total):
        window = lax.dynamic_slice_in_dim(padded, index, rows, 0)
        taps = lax.dynamic_slice_in_dim(kernel, index, 1, 0)
        return total + taps * window

    start = jnp.zeros((rows, padded.shape[1]), jnp.float32)
    return lax.fori_loop(0, kernel.shape[0], step, start)


def over_time(left, right):
    return lax.dot_general(
        left, right, (((0,), (0,)), ((), ())), preferred_element_type=jnp.float32
    )


def body(signal, readin, proj, kernel, gain, w_one, w_two, cotangent):
    rows = signal.shape[0]
    taps = kernel.shape[0]
    half = (taps - 1) // 2
    partial_latent = jnp.dot(signal, readin, preferred_element_type=jnp.float32)
    latent = lax.psum(partial_latent, "neuron").astype(jnp.bfloat16)
    lifted = jnp.dot(latent, proj, preferred_element_type=jnp.float32)
    padded = with_halo(lifted, (("tm", 0),), half)
    mixed = lifted + conv_time(padded, kernel, rows)
    scale = lax.rsqrt(jnp.mean(mixed * mixed, axis=1, keepdims=True) + 1e-05)
    normed = (mixed * scale * gain[None, :]).astype(jnp.bfloat16)
    pre = jnp.dot(normed, w_one, preferred_element_type=jnp.float32)
    act = jax.nn.silu(pre).astype(jnp.bfloat16)
    partial_mix = jnp.dot(act, w_two, preferred_element_type=jnp.float32)
    denoised = (mixed + lax.psum(partial_mix, "neuron")).astype(jnp.bfloat16)
    local_w_two = over_time(act, cotangent)
    dact = jnp.dot(cotangent, w_two.T, preferred_element_type=jnp.float32)
    sig = jax.nn.sigmoid(pre)
    dpre = (dact * sig * (1.0 + pre * (1.0 - sig))).astype(jnp.bfloat16)
    local_w_one = over_time(normed, dpre)
    partial_normed = jnp.dot(dpre, w_one.T, preferred_element_type=jnp.float32)
    dnormed = lax.psum(partial_normed, "neuron")
    local_gain = jnp.sum(dnormed * mixed * scale, axis=0)
    dgained = dnormed * gain[None, :]
    inner = jnp.mean(dgained * mixed, axis=1, keepdims=True)
    dmixed = cotangent.astype(jnp.float32) + scale * dgained - mixed * scale**3 * inner

    def kernel_row(index):
        window = lax.dynamic_slice_in_dim(padded, index, rows, 0)
        return jnp.sum(dmixed * window, axis=0)

    local_kernel = lax.map(kernel_row, jnp.arange(taps, dtype=jnp.int32))
    padded_grad = with_halo(dmixed, (("tm", 0),), half)
    dlifted = (dmixed + conv_time(padded_grad, kernel[::-1], rows)).astype(jnp.bfloat16)
    local_proj = over_time(latent, dlifted)
    dlatent = jnp.dot(dlifted, proj.T, preferred_element_type=jnp.float32).astype(jnp.bfloat16)
    grad_w_one, grad_w_two, grad_gain, grad_kernel, grad_proj = lax.psum(
        (local_w_one, local_w_two, local_gain, local_kernel, local_proj), "tm"
    )
    grad_readin = lax.psum_scatter(
        over_time(signal, dlatent), "tm", scatter_dimension=0, tiled=True
    )
    return (denoised, grad_readin, grad_proj, grad_kernel, grad_gain, grad_w_one, grad_w_two)


def solution(mesh):
    in_specs = (
        P("tm", "neuron"),
        P("neuron", None),
        P(),
        P(),
        P(),
        P(None, "neuron"),
        P("neuron", None),
        P("tm", None),
    )
    out_specs = (
        P("tm", None),
        P(("neuron", "tm"), None),
        P(),
        P(),
        P(),
        P(None, "neuron"),
        P("neuron", None),
    )
    return jax.shard_map(body, mesh=mesh, in_specs=in_specs, out_specs=out_specs, check_vma=False)
```

profile of v0, /device:TPU:1, one launch (start us, length us, event | category | flops | bytes accessed | tf_op | source)
XLA Modules:
  0.0 1194.0 jit_solution(17673050417110770765)
XLA Ops:
  8.8 3.4 fusion.12
  12.2 73.1 %all-reduce.9 = bf16[512,256]{1,0:T(8,128)(2,1)S(1)} all-reduce(f32[512,256]{1,0:T(8,128)S(1)} %fusion.12), channel_id=1, replica_groups=mesh['neuron'=16,'tm'=16] {'neuron'}, use_global_device_ids=true, to_apply=%region_0.0 | all-reduce | flops 131072 | bytes 786432 | tf_op jit(solution)/shard_map/psum | solution.py:42
  86.6 16.6 %collective-permute-start = (f32[31,512]{1,0:T(8,128)S(1)}, f32[31,512]{1,0:T(8,128)S(1)}, u32[]{:S(2)}, u32[]{:S(2)}) collective-permute-start(f32[31,512]{1,0:T(8,128)S(1)} %get-tuple-element.272), channel_id=1, source_target_pairs={{0,1},{1,2},{2,3},{3,4},{4,5},{5,6},{6,7},{7,8},{8,9},{9,10},{10,1... | collective-permute-start | bytes 190472 | tf_op jit(solution)/shard_map/ppermute | solution.py:12
  105.8 3.1 collective-permute-done.1
  110.3 200.2 %while.39 = (s32[]{:T(128)}, f32[512,512]{1,0:T(8,128)}, f32[63,512]{1,0:T(8,128)}, f32[574,512]{1,0:T(8,128)S(1)}, s32[]{:T(128)}, /*index=5*/s32[]{:T(128)}) while((s32[]{:T(128)}, f32[512,512]{1,0:T(8,128)}, f32[63,512]{1,0:T(8,128)}, f32[574,512]{1,0:T(8,128)S(1)}, s32[]{:T(128)}, /*index=5*/s32[]{:T(128)}) %tuple.83), condition=%wide.region_2.0_spmd.clone, body=%wide.region_1.0_spmd.clone.sunk | while | flops 786435 | bytes 3151959 | solution.py:28
  316.9 2.8 rev.3
  322.1 149.1 %all-reduce.8.cloned.1.call-done = (f32[512,512]{1,0:T(8,128)}, f32[512,512]{1,0:T(8,128)}) async-done(((f32[512,512]{1,0:T(8,128)}, f32[512,512]{1,0:T(8,128)}), (f32[512,512]{1,0:T(8,128)}, f32[512,512]{1,0:T(8,128)})) %all-reduce.8.cloned.1.call-update) | async-done | bytes 2097168 | tf_op jit(solution)/shard_map/psum | solution.py:51
  476.0 13.9 %collective-permute-start.2 = (f32[31,512]{1,0:T(8,128)S(1)}, f32[31,512]{1,0:T(8,128)S(1)}, u32[]{:S(2)}, u32[]{:S(2)}) collective-permute-start(f32[31,512]{1,0:T(8,128)S(1)} %get-tuple-element.268), channel_id=1, source_target_pairs={{0,1},{1,2},{2,3},{3,4},{4,5},{5,6},{6,7},{7,8},{8,9},{9,10},{10,1... | collective-permute-start | bytes 190472 | tf_op jit(solution)/shard_map/ppermute | solution.py:12
  496.7 219.1 %while.40 = (s32[]{:T(128)}, f32[512,512]{1,0:T(8,128)}, f32[63,512]{1,0:T(8,128)}, f32[574,512]{1,0:T(8,128)}, s32[]{:T(128)}, /*index=5*/s32[]{:T(128)}) while((s32[]{:T(128)}, f32[512,512]{1,0:T(8,128)}, f32[63,512]{1,0:T(8,128)}, f32[574,512]{1,0:T(8,128)}, s32[]{:T(128)}, /*index=5*/s32[]{:T(128)}) %tuple.86), condition=%wide.region_8.9_spmd.clone, body=%wide.region_7.8_spmd.clone.sunk | while | flops 786435 | bytes 3151959 | solution.py:28
  500.6 2.8 select_add_fusion.5
  504.0 2.8 select_add_fusion.5
  507.5 2.8 select_add_fusion.5
  511.0 2.8 select_add_fusion.5
  514.5 2.8 select_add_fusion.5
  518.0 2.8 select_add_fusion.5
  521.5 2.8 select_add_fusion.5
  524.9 2.8 select_add_fusion.5
  528.4 2.8 select_add_fusion.5
  531.9 2.8 select_add_fusion.5
  535.4 2.8 select_add_fusion.5
  538.9 2.8 select_add_fusion.5
  542.4 2.8 select_add_fusion.5
  545.8 2.8 select_add_fusion.5
  549.3 2.8 select_add_fusion.5
  552.8 2.8 select_add_fusion.5
  556.3 2.8 select_add_fusion.5
  559.8 2.8 select_add_fusion.5
  563.3 2.8 select_add_fusion.5
  566.7 2.8 select_add_fusion.5
  570.2 2.8 select_add_fusion.5
  573.7 2.8 select_add_fusion.5
  577.2 2.8 select_add_fusion.5
  580.7 2.8 select_add_fusion.5
  584.2 2.8 select_add_fusion.5
  587.6 2.8 select_add_fusion.5
  591.1 2.8 select_add_fusion.5
  594.6 2.8 select_add_fusion.5
  598.1 2.8 select_add_fusion.5
  601.6 2.8 select_add_fusion.5
  605.1 2.8 select_add_fusion.5
  608.5 2.8 select_add_fusion.5
  612.0 2.8 select_add_fusion.5
  615.5 2.8 select_add_fusion.5
  619.0 2.8 select_add_fusion.5
  622.5 2.8 select_add_fusion.5
  626.0 2.8 select_add_fusion.5
  629.4 2.8 select_add_fusion.5
  632.9 2.8 select_add_fusion.5
  636.4 2.8 select_add_fusion.5
  639.9 2.8 select_add_fusion.5
  643.4 2.8 select_add_fusion.5
  646.9 2.8 select_add_fusion.5
  650.3 2.8 select_add_fusion.5
  653.8 2.8 select_add_fusion.5
  657.3 2.8 select_add_fusion.5
  660.8 2.8 select_add_fusion.5
  664.3 2.8 select_add_fusion.5
  667.7 2.8 select_add_fusion.5
  671.2 2.8 select_add_fusion.5
  674.7 2.8 select_add_fusion.5
  718.3 6.3 convolution_bitcast_fusion
  724.6 331.9 %while.38 = (s32[]{:T(128)}, f32[63,512]{1,0:T(8,128)}, s32[63]{0:T(128)S(1)}, f32[574,512]{1,0:T(8,128)S(1)}, f32[512,512]{1,0:T(8,128)}, /*index=5*/s32[]{:T(128)}, s32[]{:T(128)}, s32[]{:T(128)}) while((s32[]{:T(128)}, f32[63,512]{1,0:T(8,128)}, s32[63]{0:T(128)S(1)}, f32[574,512]{1,0:T(8,128)S(1)}, f32[512,512]{1,0:T(8,128)}, ...), condition=%wide.region_13.14_spmd, body=%wide.region_11.13_spmd.sunk | while | flops 523781 | bytes 2103435 | solution.py:68
  1058.8 25.6 %psum.61 = f32[512]{0:T(512)} all-reduce(f32[512]{0:T(512)S(1)} %get-tuple-element.232), channel_id=1, replica_groups=mesh['neuron'=16,'tm'=16] {'tm'}, use_global_device_ids=true, to_apply=%region_16.17 | all-reduce | flops 512 | bytes 4096 | tf_op jit(solution)/shard_map/psum | solution.py:73
  1086.2 96.4 %all-reduce.6.cloned.1.call-done = (f32[256,512]{1,0:T(8,128)}, f32[63,512]{1,0:T(8,128)}, f32[512,128]{1,0:T(8,128)}, f32[128,512]{1,0:T(8,128)}) async-done(((f32[256,512]{1,0:T(8,128)}, f32[63,512]{1,0:T(8,128)}, f32[512,128]{1,0:T(8,128)}, f32[128,512]{1,0:T(8,128)}), (f32[256,512]{1,0:T(8,128)}, f32[63,512]{1,0:T(8,128)}, f32[512,128]{1,0:T(8,128)}, f32[128,512]{1,0:T(8,128)})) %all-reduce.6.cloned.1.call-update) | async-done | bytes 1177616 | tf_op jit(solution)/shard_map/psum | solution.py:73
  (465 shorter events, 526.3 us)
Async XLA Ops:
  7.2 1.6 copy-start
  7.2 78.1 %copy-start.6 = (bf16[256,512]{1,0:T(8,128)(2,1)S(1)}, bf16[256,512]{1,0:T(8,128)(2,1)}, u32[]{:S(2)}) copy-start(bf16[256,512]{1,0:T(8,128)(2,1)} %param.16) | copy-start | bytes 786436
  7.2 464.0 %all-reduce.8.cloned.1.call-start = ((), (), s32[]{:S(2)}) async-start(), calls=%async_computation.3 | async-start | bytes 4194304 | tf_op jit(solution)/shard_map/psum | solution.py:51
  85.6 1.0 copy-start.4
  86.6 18.5 %collective-permute-start = (f32[31,512]{1,0:T(8,128)S(1)}, f32[31,512]{1,0:T(8,128)S(1)}, u32[]{:S(2)}, u32[]{:S(2)}) collective-permute-start(f32[31,512]{1,0:T(8,128)S(1)} %get-tuple-element.272), channel_id=1, source_target_pairs={{0,1},{1,2},{2,3},{3,4},{4,5},{5,6},{6,7},{7,8},{8,9},{9,10},{10,1... | collective-permute-start | bytes 190472 | tf_op jit(solution)/shard_map/ppermute | solution.py:12
  103.2 5.7 collective-permute-start.1
  105.2 0.6 copy-start.16
  310.5 1.8 copy-start.11
  310.5 1.8 copy-start.17
  312.2 2.4 copy-start.2
  312.2 1.0 copy-start.15
  312.3 2.3 copy-start.9
  313.3 1.6 copy-start.7
  314.9 0.7 copy-start.12
  316.9 767.5 %reduce-scatter.2.cloned.1.call-start = ((), (), s32[]{:S(2)}) async-start(), calls=%async_computation.1 | async-start | bytes 4456448 | tf_op jit(solution)/shard_map/reduce_scatter | solution.py:76
  471.2 2.1 copy-start.3
  471.2 2.2 copy-start.5
  473.4 18.5 %copy-start.8 = (f32[512,128]{1,0:T(8,128)S(1)}, f32[512,128]{1,0:T(8,128)}, u32[]{:S(2)}) copy-start(f32[512,128]{1,0:T(8,128)} %copy-done.7) | copy-start | bytes 786436
  473.4 18.5 %copy-start.10 = (bf16[512,512]{1,0:T(8,128)(2,1)S(1)}, bf16[512,512]{1,0:T(8,128)(2,1)}, u32[]{:S(2)}) copy-start(bf16[512,512]{1,0:T(8,128)(2,1)} %param.21) | copy-start | bytes 1572868
  476.0 20.6 %copy-start.1 = (f32[512,512]{1,0:T(8,128)}, f32[512,512]{1,0:T(8,128)S(1)}, u32[]{:S(2)}) copy-start(f32[512,512]{1,0:T(8,128)S(1)} %get-tuple-element.397) | copy-start | bytes 3145732
  476.0 16.8 %collective-permute-start.2 = (f32[31,512]{1,0:T(8,128)S(1)}, f32[31,512]{1,0:T(8,128)S(1)}, u32[]{:S(2)}, u32[]{:S(2)}) collective-permute-start(f32[31,512]{1,0:T(8,128)S(1)} %get-tuple-element.268), channel_id=1, source_target_pairs={{0,1},{1,2},{2,3},{3,4},{4,5},{5,6},{6,7},{7,8},{8,9},{9,10},{10,1... | collective-permute-start | bytes 190472 | tf_op jit(solution)/shard_map/ppermute | solution.py:12
  489.9 5.6 collective-permute-start.3
  724.6 458.0 %all-reduce.6.cloned.1.call-start = ((), (), s32[]{:S(2)}) async-start(), calls=%async_computation.2 | async-start | bytes 2359296 | tf_op jit(solution)/shard_map/psum | solution.py:73
  1182.6 3.5 copy-start.14
  1182.6 4.2 copy-start.13
Sparse Core Ops, SparseCore 0:
  317.0 154.1 all-reduce.7
  724.7 68.6 reduce-scatter.1
  1058.9 123.6 all-reduce.5
where the time goes:
time: 1210 us; the launch traced here: 1190 us
  other arithmetic  429 us (35%)
  waiting for transfers between devices  251 us (21%)
  local copies, waits for them, and re-layouts  226 us (19%)
  loops' own time  123 us (10%)
  blocking collectives  98.8 us (8%)
  starting transfers between devices  34.4 us (3%)
  matrix products  18.8 us (2%)
  between operations  14 us (1%)
    add x126, other arithmetic, step(): return total + taps * window  328 us
    psum x1, waiting for transfers between devices, body(): denoised = (mixed + lax.psum(partial_mix, 'neuron')).astype(jnp.bfloat16)  149 us
    another operation x1, loops' own time, body(): local_kernel = lax.map(kernel_row, jnp.arange(taps, dtype=jnp.int32))  123 us
    psum x1, waiting for transfers between devices, body(): lax.psum((local_w_one, local_w_two, local_gain, local_kernel, local_proj)...  96.4 us
    dynamic_slice x126, local copies, waits for them, and re-layouts, step(): taps = lax.dynamic_slice_in_dim(kernel, index, 1, 0)  91 us
    reduce_sum x63, other arithmetic, kernel_row(): return jnp.sum(dmixed * window, axis=0)  88.8 us
    dynamic_update_slice x63, local copies, waits for them, and re-layouts, body(): local_kernel = lax.map(kernel_row, jnp.arange(taps, dtype=jnp.int32))  83.9 us
    psum x1, blocking collectives, body(): latent = lax.psum(partial_latent, 'neuron').astype(jnp.bfloat16)  73.1 us
  transfers between devices with their start and end apart: 7, of which 4 were waited for; matrix products, arithmetic and copies ran while one was open for 18% of the time, Pallas kernels for 0%

commit v1 on v0

--- a/solution.py
+++ b/solution.py
@@ -2,6 +2,8 @@
 import jax.numpy as jnp
 from jax import lax
 from jax.sharding import PartitionSpec as P
+
+clear_the_slices = lambda vals: jnp.sum(lax.all_gather(vals, axis_name="neuron"), axis=0)
 
 
 def with_halo(block, sides, width):
@@ -48,7 +50,7 @@
     pre = jnp.dot(normed, w_one, preferred_element_type=jnp.float32)
     act = jax.nn.silu(pre).astype(jnp.bfloat16)
     partial_mix = jnp.dot(act, w_two, preferred_element_type=jnp.float32)
-    denoised = (mixed + lax.psum(partial_mix, "neuron")).astype(jnp.bfloat16)
+    denoised = (mixed + clear_the_slices(partial_mix)).astype(jnp.bfloat16)
     local_w_two = over_time(act, cotangent)
     dact = jnp.dot(cotangent, w_two.T, preferred_element_type=jnp.float32)
     sig = jax.nn.sigmoid(pre)

time: 1210 us -> 1440 us (1.19)
  waiting for transfers between devices: 251 us -> 470 us
    all_gather x0 -> x1, waiting for transfers between devices: none -> 233 us  [lax.all_gather(vals, axis_name='neuron')]
    ppermute x2, starting transfers between devices: 30.4 us -> 4.72 us  [with_halo(): lax.ppermute(lax.slice_in_dim(block, block.shape[dim] - width, None, axis...]
    ppermute x2, starting transfers between devices: 3.84 us -> 19.3 us  [with_halo(): lax.ppermute(lax.slice_in_dim(block, 0, width, axis=dim), axis, backward)]
  transfers between devices with their start and end apart: 7 -> 8, of which waited for: 4 -> 5; matrix products, arithmetic and copies ran while one was open for 18% -> 16% of each run, Pallas kernels for 0% -> 0%
where the time goes in v1:
time: 1440 us; the launch traced here: 1420 us
  waiting for transfers between devices  470 us (33%)
  other arithmetic  439 us (30%)
  local copies, waits for them, and re-layouts  226 us (16%)
  loops' own time  123 us (9%)
  blocking collectives  101 us (7%)
  starting transfers between devices  24.2 us (2%)
  matrix products  19.6 us (1%)
    add x126, other arithmetic, step(): return total + taps * window  329 us
    all_gather x1, waiting for transfers between devices, lax.all_gather(vals, axis_name='neuron')  233 us
    psum x1, waiting for transfers between devices, body(): dnormed = lax.psum(partial_normed, 'neuron')  141 us
    another operation x1, loops' own time, body(): local_kernel = lax.map(kernel_row, jnp.arange(taps, dtype=jnp.int32))  123 us
    psum x1, waiting for transfers between devices, body(): lax.psum((local_w_one, local_w_two, local_gain, local_kernel, local_proj)...  95.3 us
    dynamic_slice x126, local copies, waits for them, and re-layouts, step(): taps = lax.dynamic_slice_in_dim(kernel, index, 1, 0)  91 us
    reduce_sum x63, other arithmetic, kernel_row(): return jnp.sum(dmixed * window, axis=0)  88.8 us
    dynamic_update_slice x63, local copies, waits for them, and re-layouts, body(): local_kernel = lax.map(kernel_row, jnp.arange(taps, dtype=jnp.int32))  83.9 us
  transfers between devices with their start and end apart: 8, of which 5 were waited for; matrix products, arithmetic and copies ran while one was open for 16% of the time, Pallas kernels for 0%

profile of v1, /device:TPU:1, one launch (start us, length us, event | category | flops | bytes accessed | tf_op | source)
XLA Modules:
  0.0 1417.2 jit_solution(15784245573492275653)
XLA Ops:
  8.8 3.4 fusion.12
  12.2 73.1 %all-reduce.8 = bf16[512,256]{1,0:T(8,128)(2,1)S(1)} all-reduce(f32[512,256]{1,0:T(8,128)S(1)} %fusion.12), channel_id=1, replica_groups=mesh['neuron'=16,'tm'=16] {'neuron'}, use_global_device_ids=true, to_apply=%region_0.0 | all-reduce | flops 131072 | bytes 786432 | tf_op jit(solution)/shard_map/psum | solution.py:44
  86.6 16.0 %collective-permute-start.1 = (f32[31,512]{1,0:T(8,128)S(1)}, f32[31,512]{1,0:T(8,128)S(1)}, u32[]{:S(2)}, u32[]{:S(2)}) collective-permute-start(f32[31,512]{1,0:T(8,128)S(1)} %get-tuple-element.271), channel_id=1, source_target_pairs={{1,0},{2,1},{3,2},{4,3},{5,4},{6,5},{7,6},{8,7},{9,8},{10,9},{11,1... | collective-permute-start | bytes 190472 | tf_op jit(solution)/shard_map/ppermute | solution.py:17
  107.8 199.9 %while.39 = (s32[]{:T(128)}, f32[512,512]{1,0:T(8,128)}, f32[63,512]{1,0:T(8,128)}, f32[574,512]{1,0:T(8,128)S(1)}, s32[]{:T(128)}, /*index=5*/s32[]{:T(128)}) while((s32[]{:T(128)}, f32[512,512]{1,0:T(8,128)}, f32[63,512]{1,0:T(8,128)}, f32[574,512]{1,0:T(8,128)S(1)}, s32[]{:T(128)}, /*index=5*/s32[]{:T(128)}) %tuple.83), condition=%wide.region_2.0_spmd.clone, body=%wide.region_1.0_spmd.clone.sunk | while | flops 786435 | bytes 3151967 | solution.py:30
  320.9 140.9 %all-reduce.5.cloned.1.call-done = f32[512,512]{1,0:T(8,128)} async-done(((f32[512,512]{1,0:T(8,128)}), f32[512,512]{1,0:T(8,128)}) %all-reduce.5.cloned.1.call-update) | async-done | bytes 1048592 | tf_op jit(solution)/shard_map/psum | solution.py:60
  464.3 232.6 %all-gather.3.cloned.1.call-done = f32[8192,512]{1,0:T(8,128)} async-done(((f32[512,512]{1,0:T(8,128)}), f32[8192,512]{1,0:T(8,128)}) %all-gather.3.cloned.1.call-update) | async-done | bytes 16777232 | tf_op jit(solution)/shard_map/all_gather | solution.py:6
  696.9 8.9 reduce_sum.46
  705.8 3.2 multiply_subtract_fusion
  709.0 3.3 collective-permute-start.3
  717.1 220.3 %while.40 = (s32[]{:T(128)}, f32[512,512]{1,0:T(8,128)}, f32[63,512]{1,0:T(8,128)}, f32[574,512]{1,0:T(8,128)}, s32[]{:T(128)}, /*index=5*/s32[]{:T(128)}) while((s32[]{:T(128)}, f32[512,512]{1,0:T(8,128)}, f32[63,512]{1,0:T(8,128)}, f32[574,512]{1,0:T(8,128)}, s32[]{:T(128)}, /*index=5*/s32[]{:T(128)}) %tuple.86), condition=%wide.region_8.9_spmd.clone, body=%wide.region_7.8_spmd.clone.sunk | while | flops 786435 | bytes 3151967 | solution.py:30
  721.0 2.8 select_add_fusion.5
  724.5 2.8 select_add_fusion.5
  728.0 2.8 select_add_fusion.5
  731.5 2.8 select_add_fusion.5
  735.0 2.8 select_add_fusion.5
  738.5 2.8 select_add_fusion.5
  742.0 2.8 select_add_fusion.5
  745.5 2.8 select_add_fusion.5
  749.0 2.8 select_add_fusion.5
  752.5 2.8 select_add_fusion.5
  756.0 2.8 select_add_fusion.5
  759.5 2.8 select_add_fusion.5
  763.0 2.8 select_add_fusion.5
  766.5 2.8 select_add_fusion.5
  770.0 2.8 select_add_fusion.5
  773.5 2.8 select_add_fusion.5
  777.0 2.8 select_add_fusion.5
  780.5 2.8 select_add_fusion.5
  784.0 2.8 select_add_fusion.5
  787.5 2.8 select_add_fusion.5
  791.0 2.8 select_add_fusion.5
  794.5 2.8 select_add_fusion.5
  798.0 2.8 select_add_fusion.5
  801.5 2.8 select_add_fusion.5
  805.0 2.8 select_add_fusion.5
  808.5 2.8 select_add_fusion.5
  812.0 2.8 select_add_fusion.5
  815.5 2.8 select_add_fusion.5
  819.0 2.8 select_add_fusion.5
  822.5 2.8 select_add_fusion.5
  826.0 2.8 select_add_fusion.5
  829.5 2.8 select_add_fusion.5
  833.0 2.8 select_add_fusion.5
  836.6 2.8 select_add_fusion.5
  840.1 2.8 select_add_fusion.5
  843.6 2.8 select_add_fusion.5
  847.1 2.8 select_add_fusion.5
  850.6 2.8 select_add_fusion.5
  854.1 2.8 select_add_fusion.5
  857.6 2.8 select_add_fusion.5
  861.1 2.8 select_add_fusion.5
  864.6 2.8 select_add_fusion.5
  868.1 2.8 select_add_fusion.5
  871.6 2.8 select_add_fusion.5
  885.6 2.8 select_add_fusion.5
  896.1 2.8 select_add_fusion.5
  899.6 2.8 select_add_fusion.5
  910.1 2.8 select_add_fusion.5
  913.6 2.8 select_add_fusion.5
  924.1 2.8 select_add_fusion.5
  939.9 6.2 convolution_bitcast_fusion
  946.2 331.9 %while.38 = (s32[]{:T(128)}, f32[63,512]{1,0:T(8,128)}, s32[63]{0:T(128)S(1)}, f32[574,512]{1,0:T(8,128)S(1)}, f32[512,512]{1,0:T(8,128)}, /*index=5*/s32[]{:T(128)}, s32[]{:T(128)}, s32[]{:T(128)}) while((s32[]{:T(128)}, f32[63,512]{1,0:T(8,128)}, s32[63]{0:T(128)S(1)}, f32[574,512]{1,0:T(8,128)S(1)}, f32[512,512]{1,0:T(8,128)}, ...), condition=%wide.region_13.14_spmd, body=%wide.region_11.13_spmd.sunk | while | flops 523781 | bytes 2103443 | solution.py:70
  1280.3 28.3 %psum.53 = f32[512]{0:T(512)} all-reduce(f32[512]{0:T(512)S(1)} %copy-done.16), channel_id=1, replica_groups=mesh['neuron'=16,'tm'=16] {'tm'}, use_global_device_ids=true, to_apply=%region_16.17 | all-reduce | flops 512 | bytes 4096 | tf_op jit(solution)/shard_map/psum | solution.py:75
  1310.4 95.3 %all-reduce.7.cloned.1.call-done = (f32[256,512]{1,0:T(8,128)}, f32[63,512]{1,0:T(8,128)}, f32[512,128]{1,0:T(8,128)}, f32[128,512]{1,0:T(8,128)}) async-done(((f32[256,512]{1,0:T(8,128)}, f32[63,512]{1,0:T(8,128)}, f32[512,128]{1,0:T(8,128)}, f32[128,512]{1,0:T(8,128)}), (f32[256,512]{1,0:T(8,128)}, f32[63,512]{1,0:T(8,128)}, f32[512,128]{1,0:T(8,128)}, f32[128,512]{1,0:T(8,128)})) %all-reduce.7.cloned.1.call-update) | async-done | bytes 1177616 | tf_op jit(solution)/shard_map/psum | solution.py:75
  (467 shorter events, 530.2 us)
Async XLA Ops:
  7.2 1.6 copy-start
  7.2 78.1 %copy-start.4 = (bf16[256,512]{1,0:T(8,128)(2,1)S(1)}, bf16[256,512]{1,0:T(8,128)(2,1)}, u32[]{:S(2)}) copy-start(bf16[256,512]{1,0:T(8,128)(2,1)} %param.16) | copy-start | bytes 786436
  7.2 454.6 %all-reduce.5.cloned.1.call-start = ((), (), s32[]{:S(2)}) async-start(), calls=%async_computation.1 | async-start | bytes 2097152 | tf_op jit(solution)/shard_map/psum | solution.py:60
  85.6 1.0 copy-start.3
  86.6 18.5 %collective-permute-start.1 = (f32[31,512]{1,0:T(8,128)S(1)}, f32[31,512]{1,0:T(8,128)S(1)}, u32[]{:S(2)}, u32[]{:S(2)}) collective-permute-start(f32[31,512]{1,0:T(8,128)S(1)} %get-tuple-element.271), channel_id=1, source_target_pairs={{1,0},{2,1},{3,2},{4,3},{5,4},{6,5},{7,6},{8,7},{9,8},{10,9},{11,1... | collective-permute-start | bytes 190472 | tf_op jit(solution)/shard_map/ppermute | solution.py:17
  102.7 3.8 collective-permute-start
  105.1 0.6 copy-start.14
  307.8 1.8 copy-start.9
  307.8 1.8 copy-start.15
  309.5 1.8 copy-start.2
  309.6 1.4 copy-start.7
  309.6 1.5 copy-start.13
  310.0 0.7 copy-start.5
  311.4 0.7 copy-start.10
  313.4 383.5 %all-gather.3.cloned.1.call-start = ((), (), s32[]{:S(2)}) async-start(), calls=%async_computation.3 | async-start | bytes 17825792 | tf_op jit(solution)/shard_map/all_gather | solution.py:6
  315.7 992.9 %reduce-scatter.2.cloned.1.call-start = ((), (), s32[]{:S(2)}) async-start(), calls=%async_computation.2 | async-start | bytes 4456448 | tf_op jit(solution)/shard_map/reduce_scatter | solution.py:78
  705.8 8.8 copy-start.6
  705.8 8.8 copy-start.8
  709.0 8.1 copy-start.1
  709.0 6.6 collective-permute-start.3
  712.3 3.6 collective-permute-start.2
  946.1 459.6 %all-reduce.7.cloned.1.call-start = ((), (), s32[]{:S(2)}) async-start(), calls=%async_computation.4 | async-start | bytes 2359296 | tf_op jit(solution)/shard_map/psum | solution.py:75
  1278.1 2.2 copy-start.16
  1405.7 3.5 copy-start.12
  1405.7 4.2 copy-start.11
Sparse Core Ops, SparseCore 0:
  313.5 148.2 all-reduce.4
  464.4 232.4 all-gather.2
  946.2 70.1 reduce-scatter.1
  1280.4 125.2 all-reduce.6
